TPU v7x, 256 devices: a whole 4x4x8 slice. The times are simulated.
256 devices in a mesh: docs: 32 (over y, x, z_hi), dims: 8 (over z_lo, core).
Axes of the slice: x: 4, y: 4, z: 8 (z_hi: 2, z_lo: 4; z = z_hi * 4 + z_lo), core: 2. Of those that a mesh axis runs over, the one named last changes fastest.
Arguments:
- queries: bfloat16 [16384, 3072], P('docs', 'dims'), may hold values from -6 to 6
- doc_vectors: bfloat16 [65536, 3072], P('docs', 'dims'), may hold values from -6 to 6
- surv_pairs: int32 [32, 144], P('docs'), may hold values from 0 to 2047
- surv_count: int32 [32], P('docs'), may hold values from 36 to 144, as said below
- short_pairs: int32 [32, 96], P('docs'), may hold values from 0 to 2047
- short_count: int32 [32], P('docs'), may hold values from 24 to 96, as said below
Outputs:
- prefix_scores: float32 [32, 144, 128, 128], P('docs', None, 'dims')
- full_scores: float32 [32, 96, 128, 128], P('docs', None, 'dims')
Inputs may be any that keep to these rules, and one draw needn't show every extreme that they name: `surv_count`: each shard's live survivor slots; some shard has all 144 slots live. `short_count`: each shard's live shortlist slots; some shard has all 96 slots live.
All inputs are finite; a program needn't handle non-finite values.
Results may differ from a plain program's by a relative error of at most 0.0003.
Values may be sent and summed in bfloat16 or wider, within the bound.
No kernel may reach another device: no remote copies, remote signals or barrier semaphores. Data moves between devices by JAX's collectives and lax.ppermute only.
A program may use at most 128 MiB of HBM per device.

v0:
```python
import jax
import jax.numpy as jnp
from jax import lax
from jax.sharding import PartitionSpec as P

D = 3072
PREFIX = 768
QB = 128
DB = 128


def shards(queries, doc_vectors, surv_pairs, surv_count, short_pairs, short_count):
    every_query = lax.all_gather(queries, "docs", axis=0, tiled=True)
    slice_width = queries.shape[1]
    query_blocks = every_query.reshape(-1, QB, slice_width)
    doc_blocks = doc_vectors.reshape(-1, DB, slice_width)
    local_blocks = doc_blocks.shape[0]
    columns = lax.axis_index("dims") * slice_width + jnp.arange(slice_width)
    prefix_blocks = jnp.where(
        columns[None, None, :] < PREFIX, doc_blocks, jnp.zeros((), doc_blocks.dtype)
    )

    def pair_products(pair_ids, doc_side):
        picked_queries = jnp.take(query_blocks, pair_ids // local_blocks, axis=0)
        picked_docs = jnp.take(doc_side, pair_ids % local_blocks, axis=0)
        return jnp.einsum(
            "gqc,gdc->gqd", picked_queries, picked_docs, preferred_element_type=jnp.float32
        )

    def score_slots(pair_list, doc_side):
        return pair_products(pair_list, doc_side)

    full_terms = score_slots(short_pairs[0], doc_blocks)
    prefix_terms = score_slots(surv_pairs[0], prefix_blocks)
    prefix_sum, full_sum = (
        lax.psum_scatter(prefix_terms, "dims", scatter_dimension=1, tiled=True),
        lax.psum_scatter(full_terms, "dims", scatter_dimension=1, tiled=True),
    )

    def finish(summed, live_count, factor):
        slots = jnp.arange(summed.shape[0])
        return jnp.where(slots[:, None, None] < live_count, summed * factor, jnp.float32(0.0))

    prefix_out = finish(prefix_sum, surv_count[0], float(PREFIX) ** (-0.5))
    full_out = finish(full_sum, short_count[0], float(D) ** (-0.5))
    return (prefix_out[None], full_out[None])


def solution(mesh):
    placed = (
        P("docs", "dims"),
        P("docs", "dims"),
        P("docs", None),
        P("docs"),
        P("docs", None),
        P("docs"),
    )
    return jax.shard_map(
        shards,
        mesh=mesh,
        in_specs=placed,
        out_specs=(P("docs", None, "dims", None), P("docs", None, "dims", None)),
        check_vma=False,
    )
```

profile of v0, /device:TPU:2, one launch (start us, length us, event | category | flops | bytes accessed | tf_op | source)
XLA Modules:
  0.0 420.8 jit_solution(5105553798239716115)
XLA Ops:
  7.2 0.0 all-gather.2.cloned.1.call-start
  7.2 0.7 all-gather.2.cloned.1.call-update
  7.9 0.0 reduce-scatter.5.cloned.1.call-start
  7.9 0.7 fusion.12
  8.6 0.0 copy-start.2
  8.6 9.3 %gather_fusion.3 = bf16[96,128,384]{2,1,0:T(8,128)(2,1)} fusion(bf16[16,128,384]{2,1,0:T(8,128)(2,1)} %bitcast.65, s32[1024]{0:T(1024)S(1)} %get-tuple-element.10), kind=kCustom, calls=%fused_computation.3 | custom fusion | bytes 18874752 | tf_op jit(solution)/shard_map/jit(_take)/gather | solution.py:25
  18.0 0.0 copy-done.2
  18.0 195.2 %all-gather.2.cloned.1.call-done = bf16[16384,384]{1,0:T(8,128)(2,1)} async-done(((bf16[512,384]{1,0:T(8,128)(2,1)}), bf16[16384,384]{1,0:T(8,128)(2,1)}) %all-gather.2.cloned.1.call-update) | async-done | bytes 12582928 | tf_op jit(solution)/shard_map/all_gather | solution.py:13
  213.2 12.5 %gather_fusion.2 = bf16[96,128,384]{2,1,0:T(8,128)(2,1)} fusion(bf16[128,128,384]{2,1,0:T(8,128)(2,1)} %bitcast.67, s32[1024]{0:T(1024)S(1)} %get-tuple-element.11), kind=kCustom, calls=%fused_computation.2 | custom fusion | bytes 18874752 | tf_op jit(solution)/shard_map/jit(_take)/gather | solution.py:24
  225.7 0.0 copy-start.1
  225.7 0.0 copy-start
  225.7 10.4 %fusion.5 = f32[96,128,128]{2,1,0:T(8,128)} fusion(bf16[96,128,384]{2,1,0:T(8,128)(2,1)} %gather_fusion.3, bf16[96,128,384]{2,1,0:T(8,128)(2,1)} %gather_fusion.2, pred[96]{0:T(512)(128)(4,1)S(1)} %get-tuple-element.7, pred[96]{0:T(512)(128)(4,1)S(1)} %get-tuple-element.6), kind=kOutput, calls=%fused_computation.9 | convolution fusion | flops 1217396736 | bytes 25166016 | tf_op jit(solution)/shard_map/gqc,gdc->gqd/dot_general | solution.py:26
  236.1 0.0 reduce-scatter.5.cloned.1.call-update
  236.1 0.2 reduce-scatter.3.cloned.1.call-start
  236.4 0.0 copy-done.1
  236.4 0.0 copy-done
  236.4 0.2 broadcast_select_fusion
  236.6 9.5 %gather_fusion.1 = bf16[144,128,384]{2,1,0:T(8,128)(2,1)} fusion(bf16[16,128,384]{2,1,0:T(8,128)(2,1)S(1)} %broadcast_select_fusion, s32[1024]{0:T(1024)S(1)} %pad_clamp_fusion.2), kind=kCustom, calls=%fused_computation.1 | custom fusion | bytes 28312128 | tf_op jit(solution)/shard_map/jit(_take)/gather | solution.py:25
  246.1 14.2 %gather_fusion = bf16[144,128,384]{2,1,0:T(8,128)(2,1)} fusion(bf16[128,128,384]{2,1,0:T(8,128)(2,1)} %bitcast.68, s32[1024]{0:T(1024)S(1)} %pad_clamp_fusion.3), kind=kCustom, calls=%fused_computation | custom fusion | bytes 28312128 | tf_op jit(solution)/shard_map/jit(_take)/gather | solution.py:24
  260.3 14.9 %fusion = f32[144,128,128]{2,1,0:T(8,128)} fusion(bf16[144,128,384]{2,1,0:T(8,128)(2,1)} %gather_fusion.1, bf16[144,128,384]{2,1,0:T(8,128)(2,1)} %gather_fusion, pred[144]{0:T(512)(128)(4,1)S(1)} %get-tuple-element.5, pred[144]{0:T(512)(128)(4,1)S(1)} %get-tuple-element.4), kind=kOutput, calls=%fused_computation.4 | convolution fusion | flops 1826095104 | bytes 37749024 | tf_op jit(solution)/shard_map/gqc,gdc->gqd/dot_general | solution.py:26
  275.2 0.0 reduce-scatter.3.cloned.1.call-update
  276.5 29.3 %reduce-scatter.5.cloned.1.call-done = f32[96,16,128]{2,1,0:T(8,128)} async-done(((f32[96,128,128]{2,1,0:T(8,128)}), f32[96,16,128]{2,1,0:T(8,128)}) %reduce-scatter.5.cloned.1.call-update) | async-done | bytes 786448 | tf_op jit(solution)/shard_map/reduce_scatter | solution.py:37
  305.9 2.2 select_bitcast_fusion.1
  308.0 103.7 %reduce-scatter.3.cloned.1.call-done = f32[144,16,128]{2,1,0:T(8,128)} async-done(((f32[144,128,128]{2,1,0:T(8,128)}), f32[144,16,128]{2,1,0:T(8,128)}) %reduce-scatter.3.cloned.1.call-update) | async-done | bytes 1179664 | tf_op jit(solution)/shard_map/reduce_scatter | solution.py:36
  411.8 2.5 select_bitcast_fusion
  (10 shorter events, 0.1 us)
Async XLA Ops:
  7.2 206.0 %all-gather.2.cloned.1.call-start = ((), (), s32[]{:S(2)}) async-start(), calls=%async_computation.2 | async-start | bytes 12976128 | tf_op jit(solution)/shard_map/all_gather | solution.py:13
  7.9 298.0 %reduce-scatter.5.cloned.1.call-start = ((), (), s32[]{:S(2)}) async-start(), calls=%async_computation.4 | async-start | bytes 7077888 | tf_op jit(solution)/shard_map/reduce_scatter | solution.py:37
  8.6 9.3 %copy-start.2 = (s32[1,96]{1,0:T(1,128)S(1)}, s32[1,96]{1,0:T(1,128)}, u32[]{:S(2)}) copy-start(s32[1,96]{1,0:T(1,128)} %param.10) | copy-start | bytes 1156
  225.7 10.7 %copy-start.1 = (s32[1,144]{1,0:T(1,128)S(1)}, s32[1,144]{1,0:T(1,128)}, u32[]{:S(2)}) copy-start(s32[1,144]{1,0:T(1,128)} %param.8) | copy-start | bytes 1732
  225.7 10.8 %copy-start = (bf16[2048,384]{1,0:T(8,128)(2,1)S(1)}, bf16[2048,384]{1,0:T(8,128)(2,1)}, u32[]{:S(2)}) copy-start(bf16[2048,384]{1,0:T(8,128)(2,1)} %param.7) | copy-start | bytes 4718596
  236.1 175.7 %reduce-scatter.3.cloned.1.call-start = ((), (), s32[]{:S(2)}) async-start(), calls=%async_computation.3 | async-start | bytes 10616832 | tf_op jit(solution)/shard_map/reduce_scatter | solution.py:36
Sparse Core Ops, SparseCore 0:
  11.5 201.6 all-gather.1
  236.2 69.5 reduce-scatter.4
  308.4 103.3 reduce-scatter.2
where the time goes:
time: 421 us
  waiting for transfers between devices  329 us (78%)
  local copies, waits for them, and re-layouts  45.5 us (11%)
  matrix products  25.3 us (6%)
  between operations  15.1 us (4%)
  other arithmetic  5.6 us (1%)
    all_gather x1, waiting for transfers between devices, shards(): every_query = lax.all_gather(queries, 'docs', axis=0, tiled=True)  195 us
    reduce_scatter x1, waiting for transfers between devices, shards(): lax.psum_scatter(prefix_terms, 'dims', scatter_dimension=1, tiled=True)  104 us
    reduce_scatter x1, waiting for transfers between devices, shards(): lax.psum_scatter(full_terms, 'dims', scatter_dimension=1, tiled=True)  29.3 us
    gather x2, local copies, waits for them, and re-layouts, pair_products(): picked_queries = jnp.take(query_blocks, pair_ids // local_blocks, axis=0)  26.7 us
    dot_general x2, matrix products, pair_products(): jnp.einsum('gqc,gdc->gqd', picked_queries, picked_docs, preferred_element...  25.3 us
    gather x2, local copies, waits for them, and re-layouts, pair_products(): picked_docs = jnp.take(doc_side, pair_ids % local_blocks, axis=0)  18.8 us
  transfers between devices with their start and end apart: 3, of which 3 were waited for; matrix products, arithmetic and copies ran while one was open for 12% of the time, Pallas kernels for 0%

commit v1 on v0

--- a/solution.py
+++ b/solution.py
@@ -10,7 +10,9 @@
 
 
 def shards(queries, doc_vectors, surv_pairs, surv_count, short_pairs, short_count):
-    every_query = lax.all_gather(queries, "docs", axis=0, tiled=True)
+    every_query = jnp.concatenate(
+        lax.all_to_all(jnp.stack([queries] * lax.axis_size("docs")), "docs", 0, 0), axis=0
+    )
     slice_width = queries.shape[1]
     query_blocks = every_query.reshape(-1, QB, slice_width)
     doc_blocks = doc_vectors.reshape(-1, DB, slice_width)

time: 421 us -> 592 us (1.41)
  waiting for transfers between devices: 329 us -> 481 us
  starting transfers between devices: 0.3 us -> 14.7 us
    all_to_all x0 -> x1, waiting for transfers between devices: none -> 306 us  [shards(): lax.all_to_all(jnp.stack([queries] * lax.axis_size('docs')), 'docs', 0, 0)]
    all_gather x1 -> x0, waiting for transfers between devices: 195 us -> none  [shards(): every_query = lax.all_gather(queries, 'docs', axis=0, tiled=True)]
    reduce_scatter x1, waiting for transfers between devices: 29.3 us -> 71.4 us  [shards(): lax.psum_scatter(full_terms, 'dims', scatter_dimension=1, tiled=True)]
    all_to_all x0 -> x1, starting transfers between devices: none -> 14.4 us  [shards(): lax.all_to_all(jnp.stack([queries] * lax.axis_size('docs')), 'docs', 0, 0)]
    another operation x0 -> x1, local copies, waits for them, and re-layouts: none -> 7.42 us  [shards(): jnp.stack([queries] * lax.axis_size('docs'))]
  transfers between devices with their start and end apart: 3 -> 3, of which waited for: 3 -> 3; matrix products, arithmetic and copies ran while one was open for 12% -> 8% of each run, Pallas kernels for 0% -> 0%
where the time goes in v1:
time: 592 us
  waiting for transfers between devices  481 us (81%)
  local copies, waits for them, and re-layouts  51.4 us (9%)
  matrix products  24.7 us (4%)
  between operations  15.4 us (3%)
  starting transfers between devices  14.7 us (2%)
    all_to_all x1, waiting for transfers between devices, shards(): lax.all_to_all(jnp.stack([queries] * lax.axis_size('docs')), 'docs', 0, 0)  306 us
    reduce_scatter x1, waiting for transfers between devices, shards(): lax.psum_scatter(prefix_terms, 'dims', scatter_dimension=1, tiled=True)  104 us
    reduce_scatter x1, waiting for transfers between devices, shards(): lax.psum_scatter(full_terms, 'dims', scatter_dimension=1, tiled=True)  71.4 us
    gather x2, local copies, waits for them, and re-layouts, pair_products(): picked_queries = jnp.take(query_blocks, pair_ids // local_blocks, axis=0)  26.6 us
    dot_general x2, matrix products, pair_products(): jnp.einsum('gqc,gdc->gqd', picked_queries, picked_docs, preferred_element...  24.7 us
    gather x2, local copies, waits for them, and re-layouts, pair_products(): picked_docs = jnp.take(doc_side, pair_ids % local_blocks, axis=0)  17.3 us
    all_to_all x1, starting transfers between devices, shards(): lax.all_to_all(jnp.stack([queries] * lax.axis_size('docs')), 'docs', 0, 0)  14.4 us
  transfers between devices with their start and end apart: 3, of which 3 were waited for; matrix products, arithmetic and copies ran while one was open for 8% of the time, Pallas kernels for 0%

profile of v1, /device:TPU:2, one launch (start us, length us, event | category | flops | bytes accessed | tf_op | source)
XLA Modules:
  0.0 591.9 jit_solution(18099168829980075631)
XLA Ops:
  7.2 7.4 %stack.2 = bf16[32,512,384]{2,1,0:T(8,128)(2,1)} broadcast(bf16[512,384]{1,0:T(8,128)(2,1)} %param.6), dimensions={1,2} | broadcast | bytes 12976128 | tf_op jit(solution)/shard_map/stack | solution.py:14
  14.6 0.0 copy-start.2
  14.6 0.0 copy-start
  14.6 14.4 %all-to-all-start = ((bf16[32,512,384]{2,1,0:T(8,128)(2,1)}), bf16[32,512,384]{2,1,0:T(8,128)(2,1)}, u32[]{:S(2)}, u32[]{:S(2)}) async-start(bf16[32,512,384]{2,1,0:T(8,128)(2,1)} %stack.2), calls=%async_computation | async-start | bytes 25165824 | tf_op jit(solution)/shard_map/all_to_all | solution.py:14
  29.0 0.0 reduce-scatter.5.cloned.1.call-start
  29.1 0.0 copy-done.2
  29.1 0.0 copy-done
  29.1 7.8 %gather_fusion.3 = bf16[96,128,384]{2,1,0:T(8,128)(2,1)} fusion(bf16[16,128,384]{2,1,0:T(8,128)(2,1)S(1)} %bitcast.65, s32[1024]{0:T(1024)S(1)} %get-tuple-element.10), kind=kCustom, calls=%fused_computation.3 | custom fusion | bytes 18874752 | tf_op jit(solution)/shard_map/jit(_take)/gather | solution.py:27
  37.0 305.7 %all-to-all-done = bf16[32,512,384]{2,1,0:T(8,128)(2,1)} async-done(((bf16[32,512,384]{2,1,0:T(8,128)(2,1)}), bf16[32,512,384]{2,1,0:T(8,128)(2,1)}, u32[]{:S(2)}, u32[]{:S(2)}) %all-to-all-start) | async-done | bytes 12582944 | tf_op jit(solution)/shard_map/all_to_all | solution.py:14
  342.6 12.5 %gather_fusion.2 = bf16[96,128,384]{2,1,0:T(8,128)(2,1)} fusion(bf16[128,128,384]{2,1,0:T(8,128)(2,1)} %bitcast.2, s32[1024]{0:T(1024)S(1)} %get-tuple-element.11), kind=kCustom, calls=%fused_computation.2 | custom fusion | bytes 18874752 | tf_op jit(solution)/shard_map/jit(_take)/gather | solution.py:26
  355.1 0.0 copy-start.1
  355.1 10.3 %fusion.5 = f32[96,128,128]{2,1,0:T(8,128)} fusion(bf16[96,128,384]{2,1,0:T(8,128)(2,1)} %gather_fusion.3, bf16[96,128,384]{2,1,0:T(8,128)(2,1)} %gather_fusion.2, pred[96]{0:T(512)(128)(4,1)S(1)} %get-tuple-element.7, pred[96]{0:T(512)(128)(4,1)S(1)} %get-tuple-element.6), kind=kOutput, calls=%fused_computation.9 | convolution fusion | flops 1217396736 | bytes 25166016 | tf_op jit(solution)/shard_map/gqc,gdc->gqd/dot_general | solution.py:28
  365.4 0.0 reduce-scatter.5.cloned.1.call-update
  365.4 0.2 reduce-scatter.3.cloned.1.call-start
  365.7 0.0 copy-done.1
  365.8 0.2 broadcast_select_fusion
  365.9 9.5 %gather_fusion.1 = bf16[144,128,384]{2,1,0:T(8,128)(2,1)} fusion(bf16[16,128,384]{2,1,0:T(8,128)(2,1)S(1)} %broadcast_select_fusion, s32[1024]{0:T(1024)S(1)} %pad_clamp_fusion.2), kind=kCustom, calls=%fused_computation.1 | custom fusion | bytes 28312128 | tf_op jit(solution)/shard_map/jit(_take)/gather | solution.py:27
  375.4 14.1 %gather_fusion = bf16[144,128,384]{2,1,0:T(8,128)(2,1)} fusion(bf16[128,128,384]{2,1,0:T(8,128)(2,1)} %bitcast.2, s32[1024]{0:T(1024)S(1)} %pad_clamp_fusion.3), kind=kCustom, calls=%fused_computation | custom fusion | bytes 28312128 | tf_op jit(solution)/shard_map/jit(_take)/gather | solution.py:26
  389.6 14.3 %fusion = f32[144,128,128]{2,1,0:T(8,128)} fusion(bf16[144,128,384]{2,1,0:T(8,128)(2,1)} %gather_fusion.1, bf16[144,128,384]{2,1,0:T(8,128)(2,1)} %gather_fusion, pred[144]{0:T(512)(128)(4,1)S(1)} %get-tuple-element.5, pred[144]{0:T(512)(128)(4,1)S(1)} %get-tuple-element.4), kind=kOutput, calls=%fused_computation.4 | convolution fusion | flops 1826095104 | bytes 37749024 | tf_op jit(solution)/shard_map/gqc,gdc->gqd/dot_general | solution.py:28
  403.9 0.0 reduce-scatter.3.cloned.1.call-update
  405.3 71.4 %reduce-scatter.5.cloned.1.call-done = f32[96,16,128]{2,1,0:T(8,128)} async-done(((f32[96,128,128]{2,1,0:T(8,128)}), f32[96,16,128]{2,1,0:T(8,128)}) %reduce-scatter.5.cloned.1.call-update) | async-done | bytes 786448 | tf_op jit(solution)/shard_map/reduce_scatter | solution.py:39
  476.7 2.2 select_bitcast_fusion.1
  478.9 103.7 %reduce-scatter.3.cloned.1.call-done = f32[144,16,128]{2,1,0:T(8,128)} async-done(((f32[144,128,128]{2,1,0:T(8,128)}), f32[144,16,128]{2,1,0:T(8,128)}) %reduce-scatter.3.cloned.1.call-update) | async-done | bytes 1179664 | tf_op jit(solution)/shard_map/reduce_scatter | solution.py:38
  582.6 2.5 select_bitcast_fusion
  (11 shorter events, 0.1 us)
Async XLA Ops:
  14.6 14.5 %copy-start.2 = (s32[1,96]{1,0:T(1,128)S(1)}, s32[1,96]{1,0:T(1,128)}, u32[]{:S(2)}) copy-start(s32[1,96]{1,0:T(1,128)} %param.10) | copy-start | bytes 1156
  14.6 14.5 %copy-start = (bf16[2048,384]{1,0:T(8,128)(2,1)S(1)}, bf16[2048,384]{1,0:T(8,128)(2,1)}, u32[]{:S(2)}) copy-start(bf16[2048,384]{1,0:T(8,128)(2,1)} %param.7) | copy-start | bytes 4718596
  14.6 328.0 %all-to-all-start = ((bf16[32,512,384]{2,1,0:T(8,128)(2,1)}), bf16[32,512,384]{2,1,0:T(8,128)(2,1)}, u32[]{:S(2)}, u32[]{:S(2)}) async-start(bf16[32,512,384]{2,1,0:T(8,128)(2,1)} %stack.2), calls=%async_computation | async-start | bytes 25165824 | tf_op jit(solution)/shard_map/all_to_all | solution.py:14
  29.0 447.7 %reduce-scatter.5.cloned.1.call-start = ((), (), s32[]{:S(2)}) async-start(), calls=%async_computation.4 | async-start | bytes 7077888 | tf_op jit(solution)/shard_map/reduce_scatter | solution.py:39
  355.1 10.6 %copy-start.1 = (s32[1,144]{1,0:T(1,128)S(1)}, s32[1,144]{1,0:T(1,128)}, u32[]{:S(2)}) copy-start(s32[1,144]{1,0:T(1,128)} %param.8) | copy-start | bytes 1732
  365.4 217.1 %reduce-scatter.3.cloned.1.call-start = ((), (), s32[]{:S(2)}) async-start(), calls=%async_computation.3 | async-start | bytes 10616832 | tf_op jit(solution)/shard_map/reduce_scatter | solution.py:38
Sparse Core Ops, SparseCore 0:
  365.6 111.0 reduce-scatter.4
  479.2 103.2 reduce-scatter.2
